TPU v7x, 512 devices: a whole 4x4x16 slice. The times are simulated.
512 devices in a mesh: ctx: 32 (over y_hi, z), fsdp: 16 (over y_lo, x, core).
Axes of the slice: x: 4, y: 4 (y_hi: 2, y_lo: 2; y = y_hi * 2 + y_lo), z: 16, core: 2. Of those that a mesh axis runs over, the one named last changes fastest.
Arguments:
- latents: bfloat16 [10240, 3072], P('ctx'), may hold values from -6 to 6, as said below
- timestep: int32 [1], replicated, may hold values from 0 to 999
- offsets: int32 [64], replicated, may hold values from 0 to 63, as said below
- qkv_weight: bfloat16 [3072, 16, 384], P('ctx', 'fsdp'), may hold values from -2 to 2
- mod_weight: bfloat16 [3072, 2, 256], P('ctx'), may hold values from -0.375 to 0.375
- gate_weight: bfloat16 [256, 3072], P(None, 'fsdp'), may hold values from -0.375 to 0.375
- out_weight: bfloat16 [3072, 16, 128], P('ctx', 'fsdp'), may hold values from -0.125 to 0.125
- conv_weight: bfloat16 [3, 3, 3, 3072], P(None, None, None, 'fsdp'), may hold values from -1.25 to 1.25
Outputs:
- mixed: bfloat16 [10240, 3072], P('ctx', 'fsdp')
Inputs may be any that keep to these rules, and one draw needn't show every extreme that they name: `latents`: tokens in order of frame, then row, then column. offsets[f] is at most f; the last frame's offset is exactly 63.
All inputs are finite; a program needn't handle non-finite values.
Results may differ from a plain program's by a relative error of at most 0.0095.
Values may be sent and summed in bfloat16 or wider, within the bound.
No kernel may reach another device: no remote copies, remote signals or barrier semaphores. Data moves between devices by JAX's collectives and lax.ppermute only.
A program may use at most 64 MiB of HBM per device.

v0:
```python
import math
import jax
import jax.numpy as jnp
from jax import lax
from jax.sharding import PartitionSpec as P

HH = 10
WW = 16
EPS = 1e-06
NEG = -1e30


def passed_along(block, axis, distance):
    devices = range(lax.axis_size(axis))
    route = [(i - distance, i) for i in devices if i - distance in devices]
    return lax.ppermute(block, axis, route)


def time_features(timestep, embed_width):
    half_width = embed_width // 2
    freqs = jnp.exp(-math.log(10000.0) * jnp.arange(half_width, dtype=jnp.float32) / half_width)
    angles = timestep[0].astype(jnp.float32) * freqs
    embed = jnp.concatenate([jnp.cos(angles), jnp.sin(angles)])
    return jax.nn.silu(embed).astype(jnp.bfloat16)


def attend_piece(
    state_now, kv_piece, first_key, queries, query_frame, query_first, frame_size, head_dim
):
    run_max, run_sum, accumulated = state_now
    key_count = kv_piece.shape[0]
    key_part = kv_piece[:, :, :head_dim]
    value_part = kv_piece[:, :, head_dim:]
    scores = jnp.einsum(
        "nhe,mhe->nhm", queries, key_part, preferred_element_type=jnp.float32
    ) * head_dim ** (-0.5)
    key_frame = (first_key + jnp.arange(key_count, dtype=jnp.int32)) // frame_size
    allowed = (key_frame[None, :] <= query_frame[:, None]) & (
        key_frame[None, :] >= query_first[:, None]
    )
    masked = jnp.where(allowed[:, None, :], scores, NEG)
    new_max = jnp.maximum(run_max, masked.max(-1))
    exponent = jnp.where(allowed[:, None, :], jnp.exp(masked - new_max[..., None]), 0.0)
    factor = jnp.exp(run_max - new_max)
    run_sum = run_sum * factor + exponent.sum(-1)
    accumulated = accumulated * factor[..., None] + jnp.einsum(
        "nhm,mhe->nhe",
        exponent.astype(jnp.bfloat16),
        value_part,
        preferred_element_type=jnp.float32,
    )
    return (new_max, run_sum, accumulated)


def fold_blocks(state_now, kv_piece, step_fn, block_rows):
    key_count = kv_piece.shape[0]
    split_rows = kv_piece.reshape(
        key_count // block_rows, block_rows, kv_piece.shape[1], kv_piece.shape[2]
    )

    def visit_block(state_in, block_item):
        block_no, block_rows_kv = block_item
        return (step_fn(state_in, block_rows_kv, block_no * block_rows), None)

    block_ids = jnp.arange(key_count // block_rows, dtype=jnp.int32)
    state_out, _ = lax.scan(visit_block, state_now, (block_ids, split_rows))
    return state_out


def per_device(
    latents, timestep, offsets, qkv_weight, mod_weight, gate_weight, out_weight, conv_weight
):
    tok_rows = latents.shape[0]
    heads_here = qkv_weight.shape[1]
    head_dim = out_weight.shape[2]
    chan_here = gate_weight.shape[1]
    frame_size = HH * WW
    frames_here = tok_rows // frame_size
    position = lax.axis_index("ctx")
    column = lax.axis_index("fsdp")
    time_act = time_features(timestep, gate_weight.shape[0])
    gate_vec = jnp.dot(time_act, gate_weight, preferred_element_type=jnp.float32)
    float_rows = latents.astype(jnp.float32)
    centred = float_rows - float_rows.mean(-1, keepdims=True)
    variance = (centred * centred).mean(-1, keepdims=True)
    normed = centred * lax.rsqrt(variance + EPS)
    rows_here = qkv_weight.shape[0]
    qkv_width = qkv_weight.shape[2]
    local_shares = jnp.einsum("rjt,t->rj", mod_weight, time_act, preferred_element_type=jnp.float32)
    shares_hi = local_shares.astype(jnp.bfloat16)
    shares_lo = (local_shares - shares_hi.astype(jnp.float32)).astype(jnp.bfloat16)
    bundle = jnp.concatenate(
        [
            qkv_weight.reshape(rows_here, heads_here * qkv_width),
            out_weight.reshape(rows_here, heads_here * head_dim),
            shares_hi,
            shares_lo,
        ],
        axis=1,
    )
    gathered = lax.all_gather(bundle, "ctx", axis=0, tiled=True)
    full_rows = gathered.shape[0]
    qkv_cols = heads_here * qkv_width
    out_cols = heads_here * head_dim
    w_piece = gathered[:, :qkv_cols].reshape(full_rows, heads_here, qkv_width)
    o_piece = gathered[:, qkv_cols : qkv_cols + out_cols].reshape(full_rows, heads_here, head_dim)
    share_bits = gathered[:, qkv_cols + out_cols :].astype(jnp.float32)
    shares = share_bits[:, :2] + share_bits[:, 2:]
    modulated = (normed * (1.0 + shares[:, 1]) + shares[:, 0]).astype(jnp.bfloat16)
    projected_qkv = jnp.einsum(
        "nr,rhc->nhc", modulated, w_piece, preferred_element_type=jnp.float32
    ).astype(jnp.bfloat16)
    queries = projected_qkv[:, :, :head_dim]
    packed = projected_qkv[:, :, head_dim:]
    query_frame = position * frames_here + jnp.arange(tok_rows, dtype=jnp.int32) // frame_size
    local_first = lax.dynamic_slice_in_dim(offsets, position * frames_here, frames_here, 0)
    query_first = jnp.repeat(local_first, frame_size)
    start_state = (
        jnp.full((tok_rows, heads_here), NEG, jnp.float32),
        jnp.zeros((tok_rows, heads_here), jnp.float32),
        jnp.zeros((tok_rows, heads_here, head_dim), jnp.float32),
    )
    block_rows = 2 * tok_rows

    def attend(state_now, kv_piece, first_key):
        return attend_piece(
            state_now, kv_piece, first_key, queries, query_frame, query_first, frame_size, head_dim
        )

    run_max, run_sum, accumulated = fold_blocks(
        start_state, lax.all_gather(packed, "ctx", axis=0, tiled=True), attend, block_rows
    )
    attended = (accumulated / run_sum[..., None]).astype(jnp.bfloat16)
    partial_out = jnp.einsum("nhe,rhe->nr", attended, o_piece, preferred_element_type=jnp.float32)
    head_total = lax.psum_scatter(
        partial_out.astype(jnp.bfloat16), "fsdp", scatter_dimension=1, tiled=True
    ).astype(jnp.float32)
    own_chan = lax.dynamic_slice_in_dim(latents, column * chan_here, chan_here, 1)
    before = passed_along(own_chan, "ctx", 1)
    stacked = (
        jnp.concatenate([before, own_chan], 0)
        .astype(jnp.float32)
        .reshape(frames_here + 2, HH, WW, chan_here)
    )
    padded = jnp.pad(stacked, ((0, 0), (1, 1), (1, 1), (0, 0)))
    convolved = jnp.zeros((frames_here, HH, WW, chan_here), jnp.float32)
    for time_lag in range(3):
        for row_shift in range(3):
            for col_shift in range(3):
                tap = conv_weight[time_lag, row_shift, col_shift].astype(jnp.float32)
                convolved = (
                    convolved
                    + tap
                    * padded[
                        2 - time_lag : 2 - time_lag + frames_here,
                        row_shift : row_shift + HH,
                        col_shift : col_shift + WW,
                    ]
                )
    residual = own_chan.astype(jnp.float32)
    mixed = residual + gate_vec * head_total + convolved.reshape(tok_rows, chan_here)
    return mixed.astype(jnp.bfloat16)


def solution(mesh):
    in_specs = (
        P("ctx", None),
        P(),
        P(),
        P("ctx", "fsdp", None),
        P("ctx", None, None),
        P(None, "fsdp"),
        P("ctx", "fsdp", None),
        P(None, None, None, "fsdp"),
    )
    out_specs = P("ctx", "fsdp")
    return jax.shard_map(
        per_device, mesh=mesh, in_specs=in_specs, out_specs=out_specs, check_vma=False
    )
```

profile of v0, /device:TPU:32, one launch (start us, length us, event | category | flops | bytes accessed | tf_op | source)
XLA Modules:
  0.0 485.3 jit_solution(17367744901689047)
XLA Ops:
  7.9 1.6 pad_maximum_fusion
  9.6 1.9 convert_reduce_fusion
  11.5 0.7 fusion.28
  12.2 165.2 %all-gather.3.cloned.1.call-done = bf16[3072,516]{1,0:T(8,128)(2,1)} async-done(((bf16[96,516]{1,0:T(8,128)(2,1)}), bf16[3072,516]{1,0:T(8,128)(2,1)}) %all-gather.3.cloned.1.call-update) | async-done | bytes 3170320 | tf_op jit(solution)/shard_map/all_gather | solution.py:101
  177.3 1.2 slice_convert_fusion
  179.1 1.3 fusion.39
  180.7 1.3 fusion.45
  181.9 0.7 slice.289
  182.8 166.0 %all-gather.5.cloned.1.call-done = bf16[10240,1,256]{2,0,1:T(8,128)(2,1)} async-done(((bf16[320,1,256]{2,0,1:T(8,128)(2,1)}), bf16[10240,1,256]{2,0,1:T(8,128)(2,1)}) %all-gather.5.cloned.1.call-update) | async-done | bytes 5242896 | tf_op jit(solution)/shard_map/all_gather | solution.py:131
  348.9 58.9 %while.17 = (s32[]{:T(128)}, f32[320,1]{0,1:T(1,128)S(1)}, f32[320,1]{0,1:T(1,128)S(1)}, f32[320,1,128]{2,0,1:T(8,128)S(1)}, s32[16]{0:T(128)S(1)}, /*index=5*/b...) while((s32[]{:T(128)}, f32[320,1]{0,1:T(1,128)S(1)}, ...), condition=%wide.region_5.6_spmd.clone, body=%wide.region_2.5_spmd.clone.sunk | while | flops 108677440 | bytes 3902893 | solution.py:66
  350.0 1.0 dynamic-slice_bitcast_fusion.2
  353.7 1.0 dynamic-slice_bitcast_fusion.2
  357.4 1.0 dynamic-slice_bitcast_fusion.2
  361.1 1.0 dynamic-slice_bitcast_fusion.2
  364.8 1.0 dynamic-slice_bitcast_fusion.2
  368.5 1.0 dynamic-slice_bitcast_fusion.2
  372.1 1.0 dynamic-slice_bitcast_fusion.2
  375.8 1.0 dynamic-slice_bitcast_fusion.2
  379.5 1.0 dynamic-slice_bitcast_fusion.2
  383.2 1.0 dynamic-slice_bitcast_fusion.2
  386.9 1.0 dynamic-slice_bitcast_fusion.2
  390.5 1.0 dynamic-slice_bitcast_fusion.2
  394.2 1.0 dynamic-slice_bitcast_fusion.2
  397.9 1.0 dynamic-slice_bitcast_fusion.2
  401.6 1.0 dynamic-slice_bitcast_fusion.2
  405.3 1.0 dynamic-slice_bitcast_fusion.2
  407.8 3.4 convolution_convert_fusion
  411.5 2.3 collective-permute-start
  414.0 4.5 collective-permute-done
  419.6 0.8 fusion.96
  420.5 56.5 %reduce-scatter.2.cloned.1.call-done = bf16[320,192]{0,1:T(8,128)(2,1)} async-done(((bf16[320,3072]{0,1:T(8,128)(2,1)}), bf16[320,192]{0,1:T(8,128)(2,1)}) %reduce-scatter.2.cloned.1.call-update) | async-done | bytes 122896 | tf_op jit(solution)/shard_map/reduce_scatter | solution.py:135
  477.0 1.7 add_convert_fusion
  (224 shorter events, 36.0 us)
Async XLA Ops:
  6.5 0.9 copy-start
  6.5 5.0 %copy-start.1 = (bf16[320,3072]{1,0:T(8,128)(2,1)S(1)}, bf16[320,3072]{1,0:T(8,128)(2,1)}, u32[]{:S(2)}) copy-start(bf16[320,3072]{1,0:T(8,128)(2,1)} %param.10) | copy-start | bytes 5898244
  6.5 170.8 %all-gather.3.cloned.1.call-start = ((), (), s32[]{:S(2)}) async-start(), calls=%async_computation.1 | async-start | bytes 4055040 | tf_op jit(solution)/shard_map/all_gather | solution.py:101
  9.5 339.3 %all-gather.5.cloned.1.call-start = ((), (), s32[]{:S(2)}) async-start(), calls=%async_computation.2 | async-start | bytes 5406720 | tf_op jit(solution)/shard_map/all_gather | solution.py:131
  178.6 2.1 copy-start.2
  180.7 2.1 copy-start.5
  182.7 294.4 %reduce-scatter.2.cloned.1.call-start = ((), (), s32[]{:S(2)}) async-start(), calls=%async_computation.3 | async-start | bytes 2506752 | tf_op jit(solution)/shard_map/reduce_scatter | solution.py:135
  411.2 2.7 copy-start.4
  411.2 2.7 copy-start.3
  411.5 7.0 %collective-permute-start = (bf16[320,192]{0,1:T(8,128)(2,1)S(1)}, bf16[320,192]{0,1:T(8,128)(2,1)S(1)}, u32[]{:S(2)}, u32[]{:S(2)}) collective-permute-start(bf16[320,192]{0,1:T(8,128)(2,1)S(1)} %copy.30), channel_id=1, source_target_pairs={{0,16},{16,32},{32,48},{48,64},{64,80},{80,96},{96,112},{112,128},... | collective-permute-start | bytes 368648 | tf_op jit(solution)/shard_map/ppermute | solution.py:16
Sparse Core Ops, SparseCore 0:
  10.5 166.8 all-gather.2
  182.8 166.0 all-gather.4
  411.3 65.6 reduce-scatter.1
where the time goes:
time: 487 us; the launch traced here: 485 us
  waiting for transfers between devices  392 us (80%)
  local copies, waits for them, and re-layouts  30.7 us (6%)
  matrix products  18.5 us (4%)
  other arithmetic  17.3 us (4%)
  between operations  14.2 us (3%)
  loops' own time  10 us (2%)
    all_gather x1, waiting for transfers between devices, per_device(): lax.all_gather(packed, 'ctx', axis=0, tiled=True)  166 us
    all_gather x1, waiting for transfers between devices, per_device(): gathered = lax.all_gather(bundle, 'ctx', axis=0, tiled=True)  165 us
    reduce_scatter x1, waiting for transfers between devices, per_device(): lax.psum_scatter(partial_out.astype(jnp.bfloat16), 'fsdp', scatter_dimens...  56.5 us
    squeeze x16, local copies, waits for them, and re-layouts, fold_blocks(): state_out, _ = lax.scan(visit_block, state_now, (block_ids, split_rows))  16 us
    another operation x1, loops' own time, fold_blocks(): state_out, _ = lax.scan(visit_block, state_now, (block_ids, split_rows))  10 us
  transfers between devices with their start and end apart: 4, of which 4 were waited for; matrix products, arithmetic and copies ran while one was open for 1% of the time, Pallas kernels for 0%

commit v1 on v0

--- a/solution.py
+++ b/solution.py
@@ -128,7 +128,12 @@
         )
 
     run_max, run_sum, accumulated = fold_blocks(
-        start_state, lax.all_gather(packed, "ctx", axis=0, tiled=True), attend, block_rows
+        start_state,
+        jnp.concatenate(
+            lax.all_to_all(jnp.stack([packed] * lax.psum(1, "ctx")), "ctx", 0, 0), axis=0
+        ),
+        attend,
+        block_rows,
     )
     attended = (accumulated / run_sum[..., None]).astype(jnp.bfloat16)
     partial_out = jnp.einsum("nhe,rhe->nr", attended, o_piece, preferred_element_type=jnp.float32)

time: 487 us -> 556 us (1.14)
  the two profiles are of different devices: /device:TPU:32 before, /device:TPU:16 now
where the time goes in v1:
time: 556 us; the launch traced here: 555 us
  waiting for transfers between devices  442 us (79%)
  local copies, waits for them, and re-layouts  33.3 us (6%)
  starting transfers between devices  18.8 us (3%)
  matrix products  18.5 us (3%)
  other arithmetic  17.3 us (3%)
  between operations  14.5 us (3%)
  loops' own time  11 us (2%)
    all_to_all x1, waiting for transfers between devices, per_device(): lax.all_to_all(jnp.stack([packed] * lax.psum(1, 'ctx')), 'ctx', 0, 0)  220 us
    all_gather x1, waiting for transfers between devices, per_device(): gathered = lax.all_gather(bundle, 'ctx', axis=0, tiled=True)  162 us
    reduce_scatter x1, waiting for transfers between devices, per_device(): lax.psum_scatter(partial_out.astype(jnp.bfloat16), 'fsdp', scatter_dimens...  57.3 us
    squeeze x16, local copies, waits for them, and re-layouts, fold_blocks(): state_out, _ = lax.scan(visit_block, state_now, (block_ids, split_rows))  16 us
  transfers between devices with their start and end apart: 4, of which 4 were waited for; matrix products, arithmetic and copies ran while one was open for 1% of the time, Pallas kernels for 0%

profile of v1, /device:TPU:16, one launch (start us, length us, event | category | flops | bytes accessed | tf_op | source)
XLA Modules:
  0.0 555.1 jit_solution(15145927185033398160)
XLA Ops:
  7.9 1.6 pad_maximum_fusion
  9.5 1.9 convert_reduce_fusion
  12.1 162.4 %all-gather.2.cloned.1.call-done = bf16[3072,516]{1,0:T(8,128)(2,1)} async-done(((bf16[96,516]{1,0:T(8,128)(2,1)}), bf16[3072,516]{1,0:T(8,128)(2,1)}) %all-gather.2.cloned.1.call-update) | async-done | bytes 3170320 | tf_op jit(solution)/shard_map/all_gather | solution.py:101
  174.6 1.2 slice_convert_fusion
  176.3 1.3 fusion.39
  177.9 1.3 fusion.45
  179.2 2.9 stack.2
  182.1 10.8 %all-to-all-start = ((bf16[32,320,1,256]{3,1,2,0:T(8,128)(2,1)}), bf16[32,320,1,256]{3,1,2,0:T(8,128)(2,1)}, u32[]{:S(2)}, u32[]{:S(2)}) async-start(bf16[32,320,1,256]{3,1,2,0:T(8,128)(2,1)} %stack.2), calls=%async_computation | async-start | bytes 10485760 | tf_op jit(solution)/shard_map/all_to_all | solution.py:133
  193.2 219.5 %all-to-all-done = bf16[32,320,1,256]{3,1,2,0:T(8,128)(2,1)} async-done(((bf16[32,320,1,256]{3,1,2,0:T(8,128)(2,1)}), bf16[32,320,1,256]{3,1,2,0:T(8,128)(2,1)}, u32[]{:S(2)}, u32[]{:S(2)}) %all-to-all-start) | async-done | bytes 5242912 | tf_op jit(solution)/shard_map/all_to_all | solution.py:133
  412.7 60.2 %while.17 = (s32[]{:T(128)}, f32[320,1]{0,1:T(1,128)S(1)}, f32[320,1]{0,1:T(1,128)S(1)}, f32[320,1,128]{2,0,1:T(8,128)S(1)}, s32[16]{0:T(128)S(1)}, /*index=5*/b...) while((s32[]{:T(128)}, f32[320,1]{0,1:T(1,128)S(1)}, ...), condition=%wide.region_5.6_spmd.clone, body=%wide.region_2.5_spmd.clone.sunk | while | flops 108677440 | bytes 3902893 | solution.py:66
  414.0 1.0 dynamic-slice_bitcast_fusion.2
  417.7 1.0 dynamic-slice_bitcast_fusion.2
  421.5 1.0 dynamic-slice_bitcast_fusion.2
  425.3 1.0 dynamic-slice_bitcast_fusion.2
  429.0 1.0 dynamic-slice_bitcast_fusion.2
  432.8 1.0 dynamic-slice_bitcast_fusion.2
  436.5 1.0 dynamic-slice_bitcast_fusion.2
  440.3 1.0 dynamic-slice_bitcast_fusion.2
  444.1 1.0 dynamic-slice_bitcast_fusion.2
  447.8 1.0 dynamic-slice_bitcast_fusion.2
  451.6 1.0 dynamic-slice_bitcast_fusion.2
  455.3 1.0 dynamic-slice_bitcast_fusion.2
  459.1 1.0 dynamic-slice_bitcast_fusion.2
  462.9 1.0 dynamic-slice_bitcast_fusion.2
  466.6 1.0 dynamic-slice_bitcast_fusion.2
  470.4 1.0 dynamic-slice_bitcast_fusion.2
  472.9 3.4 convolution_convert_fusion
  476.6 8.0 %collective-permute-start = (bf16[320,192]{0,1:T(8,128)(2,1)S(1)}, bf16[320,192]{0,1:T(8,128)(2,1)S(1)}, u32[]{:S(2)}, u32[]{:S(2)}) collective-permute-start(bf16[320,192]{0,1:T(8,128)(2,1)S(1)} %copy.36), channel_id=1, source_target_pairs={{0,16},{16,32},{32,48},{48,64},{64,80},{80,96},{96,112},{112,128},... | collective-permute-start | bytes 368648 | tf_op jit(solution)/shard_map/ppermute | solution.py:16
  484.8 2.4 collective-permute-done
  488.3 0.8 fusion.96
  489.3 57.3 %reduce-scatter.2.cloned.1.call-done = bf16[320,192]{0,1:T(8,128)(2,1)} async-done(((bf16[320,3072]{0,1:T(8,128)(2,1)}), bf16[320,192]{0,1:T(8,128)(2,1)}) %reduce-scatter.2.cloned.1.call-update) | async-done | bytes 122896 | tf_op jit(solution)/shard_map/reduce_scatter | solution.py:140
  546.6 1.7 add_convert_fusion
  (224 shorter events, 36.9 us)
Async XLA Ops:
  6.5 0.9 copy-start
  6.5 4.9 copy-start.1
  6.5 168.0 %all-gather.2.cloned.1.call-start = ((), (), s32[]{:S(2)}) async-start(), calls=%async_computation.2 | async-start | bytes 4055040 | tf_op jit(solution)/shard_map/all_gather | solution.py:101
  175.8 2.1 copy-start.2
  182.1 10.9 %copy-start.5 = (s32[64]{0:T(128)S(1)}, s32[64]{0:T(128)}, u32[]{:S(2)}) copy-start(s32[64]{0:T(128)} %param.12) | copy-start | bytes 772
  182.1 230.6 %all-to-all-start = ((bf16[32,320,1,256]{3,1,2,0:T(8,128)(2,1)}), bf16[32,320,1,256]{3,1,2,0:T(8,128)(2,1)}, u32[]{:S(2)}, u32[]{:S(2)}) async-start(bf16[32,320,1,256]{3,1,2,0:T(8,128)(2,1)} %stack.2), calls=%async_computation | async-start | bytes 10485760 | tf_op jit(solution)/shard_map/all_to_all | solution.py:133
  193.0 353.6 %reduce-scatter.2.cloned.1.call-start = ((), (), s32[]{:S(2)}) async-start(), calls=%async_computation.3 | async-start | bytes 2506752 | tf_op jit(solution)/shard_map/reduce_scatter | solution.py:140
  476.3 8.3 %copy-start.4 = (bf16[3,3,3,192]{3,2,1,0:T(4,128)(2,1)S(1)}, bf16[3,3,3,192]{3,2,1,0:T(4,128)(2,1)}, u32[]{:S(2)}) copy-start(bf16[3,3,3,192]{3,2,1,0:T(4,128)(2,1)} %param.17) | copy-start | bytes 31108
  476.3 8.3 %copy-start.3 = (bf16[256,192]{0,1:T(8,128)(2,1)S(1)}, bf16[256,192]{0,1:T(8,128)(2,1)}, u32[]{:S(2)}) copy-start(bf16[256,192]{0,1:T(8,128)(2,1)} %param.15) | copy-start | bytes 294916
  476.6 10.7 %collective-permute-start = (bf16[320,192]{0,1:T(8,128)(2,1)S(1)}, bf16[320,192]{0,1:T(8,128)(2,1)S(1)}, u32[]{:S(2)}, u32[]{:S(2)}) collective-permute-start(bf16[320,192]{0,1:T(8,128)(2,1)S(1)} %copy.36), channel_id=1, source_target_pairs={{0,16},{16,32},{32,48},{48,64},{64,80},{80,96},{96,112},{112,128},... | collective-permute-start | bytes 368648 | tf_op jit(solution)/shard_map/ppermute | solution.py:16
Sparse Core Ops, SparseCore 0:
  10.5 164.0 all-gather.1
  476.5 70.0 reduce-scatter.1
